TPU v7x, 256 devices: a whole 4x4x8 slice. The times are simulated.
256 devices in a mesh: section: 2 (over core), req: 32 (over z, y), head: 4 (over x).
Axes of the slice: x: 4, y: 4, z: 8, core: 2. Of those that a mesh axis runs over, the one named last changes fastest.
Arguments:
- token_ids: int32 [128, 4], P('req'), may hold values from 0 to 31999
- request_order: int32 [128], replicated, may hold values from 0 to 127, each once
- window_lengths: int32 [128], replicated, may hold values from 1 to 512, as said below
- embed_table: bfloat16 [32000, 2048], P(('req', 'head')), may hold values from -6 to 6
- cache_arrived: bfloat16 [2, 128, 512, 2, 2048], P('section', None, 'req', None, 'head'), may hold values from -16 to 16
- state_arrived: float32 [2, 128, 128, 16, 128], P('section', None, 'req', 'head'), may hold values from -2 to 2
- conv_history: bfloat16 [2, 128, 3, 3, 2048], P('section', 'req', None, None, 'head'), may hold values from -6 to 6
- sink_cache: bfloat16 [2, 128, 4, 2, 2048], P('section', 'req', None, None, 'head'), may hold values from -16 to 16
- w_qkv: bfloat16 [2, 2048, 3, 2048], P('section', None, None, 'head'), may hold values from -0.125 to 0.125
- w_out: bfloat16 [2, 2048, 2048], P('section', 'head'), may hold values from -0.125 to 0.125
- w_beta: bfloat16 [2, 2048, 16], P('section', None, 'head'), may hold values from -0.125 to 0.125
- conv_taps: float32 [2, 4, 3, 2048], P('section', None, None, 'head'), may hold values from -3 to 3
- pre_gain: float32 [2, 2048], P('section'), may hold values from 0.25 to 1.75
- out_gain: float32 [2, 2048], P('section', 'head'), may hold values from 0.25 to 1.75
- score_scale_table: float32 [2, 16], P('section', 'head'), may hold values from 4 to 512
Outputs:
- layer_out: bfloat16 [2, 128, 4, 2048], P('section', 'req')
- final_state: float32 [2, 128, 128, 16, 128], P('section', 'req', None, 'head')
Inputs may be any that keep to these rules, and one draw needn't show every extreme that they name: `request_order`: a permutation of the arriving requests. `window_lengths`: some request holds a full window.
All inputs are finite; a program needn't handle non-finite values.
Results may differ from a plain program's by a relative error of at most 0.025.
Values may be sent and summed in bfloat16 or wider, within the bound.
No kernel may reach another device: no remote copies, remote signals or barrier semaphores. Data moves between devices by JAX's collectives and lax.ppermute only.
A program may use at most 128 MiB of HBM per device.

v0:
```python
import jax
import jax.numpy as jnp
from jax import lax
from jax.sharding import PartitionSpec as P

WIN = 512
epsilon = 1e-06
negative_big = -1e30


def passed_along(value, axis, by):
    peers = lax.axis_size(axis)
    pairs = [(i, i + by) for i in range(peers) if 0 <= i + by < peers]
    return lax.ppermute(value, axis, pairs)


def rms_scale(values, gain_row):
    return (
        values * lax.rsqrt(jnp.mean(values * values, axis=-1, keepdims=True) + epsilon) * gain_row
    )


def unit_rows(values):
    return values * lax.rsqrt(jnp.sum(values * values, axis=-1, keepdims=True) + epsilon)


def shards(
    token_ids,
    request_order,
    window_lengths,
    embed_table,
    cache_arrived,
    state_arrived,
    conv_history,
    sink_cache,
    w_qkv,
    w_out,
    w_beta,
    conv_taps,
    pre_gain,
    out_gain,
    score_scale_table,
):
    slot_count, token_count = token_ids.shape
    heads_dev = score_scale_table.shape[1]
    width = pre_gain.shape[1]
    local_width = out_gain.shape[1]
    head_dim = local_width // heads_dev
    group_index = lax.axis_index("req")
    section_index = lax.axis_index("section")
    vocab_dev = embed_table.shape[0]
    all_ids = lax.all_gather(token_ids, "req", axis=0, tiled=True)
    first_row = lax.axis_index(("req", "head")) * vocab_dev
    onehot = (
        all_ids.reshape(-1)[:, None] == first_row + jnp.arange(vocab_dev, dtype=jnp.int32)[None, :]
    ).astype(jnp.bfloat16)
    looked_up = jnp.dot(onehot, embed_table, preferred_element_type=jnp.float32)
    summed = lax.psum(looked_up, ("req", "head"))
    own_rows = lax.dynamic_slice_in_dim(
        summed, group_index * slot_count * token_count, slot_count * token_count, 0
    )
    embedded = own_rows.astype(jnp.bfloat16).reshape(slot_count, token_count, width)
    ordered_states = jnp.take(state_arrived, request_order, axis=1)
    delta_state = lax.all_to_all(ordered_states, "req", split_axis=1, concat_axis=2, tiled=True)[0]
    ordered_cache = jnp.take(cache_arrived, request_order, axis=1)
    all_lengths = jnp.take(window_lengths, request_order)
    own_lengths = lax.dynamic_slice_in_dim(all_lengths, group_index * slot_count, slot_count, 0)
    window_cache = lax.all_to_all(ordered_cache, "req", split_axis=1, concat_axis=2, tiled=True)[0]
    cache_rows = window_cache.shape[1]
    cache_holders = window_cache.shape[0]
    stored_key_rows = window_cache[:, :, 0].reshape(cache_holders, cache_rows, heads_dev, head_dim)
    cache_values = window_cache[:, :, 1].reshape(cache_holders, cache_rows, heads_dev, head_dim)
    sink_count = sink_cache.shape[2]
    anchor_key_rows = sink_cache[0][:, :, 0].reshape(slot_count, sink_count, heads_dev, head_dim)
    sink_values = sink_cache[0][:, :, 1].reshape(slot_count, sink_count, heads_dev, head_dim)
    qkv_matrix = w_qkv[0].reshape(width, 3 * local_width)
    conv_weights = conv_taps[0]
    softmax_scale_factor = score_scale_table[0]
    gain_head = out_gain[0].reshape(heads_dev, head_dim)
    new_index = jnp.arange(token_count, dtype=jnp.int32)
    row_index = jnp.arange(cache_rows, dtype=jnp.int32)
    history = conv_history[0]
    new_keys = jnp.zeros((slot_count, token_count, heads_dev, head_dim), jnp.bfloat16)
    new_values = jnp.zeros((slot_count, token_count, heads_dev, head_dim), jnp.bfloat16)
    received = jnp.zeros((slot_count, width), jnp.bfloat16)
    produced = jnp.zeros((slot_count, token_count, width), jnp.bfloat16)
    for position in range(token_count + 1):
        t_raw = position - section_index
        is_valid = (t_raw >= 0) & (t_raw < token_count)
        t_index = jnp.clip(t_raw, 0, token_count - 1)
        fresh_input = embedded[:, min(position, token_count - 1)]
        stream_in = jnp.where(section_index == 0, fresh_input, received)
        mixer_history = history
        mixer_delta_state = delta_state
        mixer_new_keys = new_keys
        mixer_new_values = new_values
        normed = rms_scale(stream_in.astype(jnp.float32), pre_gain[0]).astype(jnp.bfloat16)
        projected = (
            jnp.dot(normed, qkv_matrix, preferred_element_type=jnp.float32)
            .astype(jnp.bfloat16)
            .reshape(slot_count, 3, local_width)
        )
        conv_window = jnp.concatenate([mixer_history, projected[:, None]], axis=1)
        activated = jax.nn.silu(
            jnp.sum(conv_window.astype(jnp.float32) * conv_weights[None], axis=1)
        )
        query_vec = unit_rows(activated[:, 0].reshape(slot_count, heads_dev, head_dim))
        key_vec = unit_rows(activated[:, 1].reshape(slot_count, heads_dev, head_dim))
        value_vec = activated[:, 2].reshape(slot_count, heads_dev, head_dim)
        beta_gate = jax.nn.sigmoid(jnp.dot(normed, w_beta[0], preferred_element_type=jnp.float32))
        predicted = jnp.einsum(
            "skhv,shk->shv", mixer_delta_state, key_vec, precision=lax.Precision.HIGHEST
        )
        update = jnp.transpose(key_vec, (0, 2, 1))[:, :, :, None] * (value_vec - predicted)[:, None]
        mixer_delta_state = mixer_delta_state + beta_gate[:, None, :, None] * update
        readout = jnp.einsum(
            "skhv,shk->shv", mixer_delta_state, query_vec, precision=lax.Precision.HIGHEST
        )
        query_halfwidth = query_vec.astype(jnp.bfloat16)
        mixer_new_keys = lax.dynamic_update_slice_in_dim(
            mixer_new_keys, key_vec.astype(jnp.bfloat16)[:, None], t_index, 1
        )
        mixer_new_values = lax.dynamic_update_slice_in_dim(
            mixer_new_values, value_vec.astype(jnp.bfloat16)[:, None], t_index, 1
        )
        anchor_score_rows = (
            jnp.einsum(
                "kry,kgry->krg",
                query_halfwidth,
                anchor_key_rows,
                preferred_element_type=jnp.float32,
            )
            * softmax_scale_factor[None, :, None]
        )
        incoming_score_rows = (
            jnp.einsum(
                "kry,kgry->krg", query_halfwidth, mixer_new_keys, preferred_element_type=jnp.float32
            )
            * softmax_scale_factor[None, :, None]
        )
        fresh_mask = (new_index <= t_index)[None, None, :]
        home_max = jnp.maximum(
            jnp.max(anchor_score_rows, axis=-1),
            jnp.max(jnp.where(fresh_mask, incoming_score_rows, negative_big), axis=-1),
        )
        limit = jnp.maximum(WIN - own_lengths, t_index + 1)
        cache_mask = row_index[None, None, :] >= limit[:, None, None]
        stored_score_rows = (
            jnp.einsum(
                "xqa,xeqa->xqe",
                query_halfwidth,
                stored_key_rows,
                preferred_element_type=jnp.float32,
            )
            * softmax_scale_factor[None, :, None]
        )
        highest = jnp.maximum(
            home_max, jnp.max(jnp.where(cache_mask, stored_score_rows, negative_big), axis=-1)
        )
        cache_weights = jnp.where(cache_mask, jnp.exp(stored_score_rows - highest[:, :, None]), 0.0)
        cache_sum = jnp.sum(cache_weights, axis=-1)
        cache_part = jnp.einsum(
            "shw,swhd->shd",
            cache_weights.astype(jnp.bfloat16),
            cache_values,
            preferred_element_type=jnp.float32,
        )
        sink_weights = jnp.exp(anchor_score_rows - highest[:, :, None])
        fresh_weights = jnp.where(
            fresh_mask, jnp.exp(incoming_score_rows - highest[:, :, None]), 0.0
        )
        weight_sum = cache_sum + jnp.sum(sink_weights, axis=-1) + jnp.sum(fresh_weights, axis=-1)
        numerator = cache_part + jnp.einsum(
            "shj,sjhd->shd",
            sink_weights.astype(jnp.bfloat16),
            sink_values,
            preferred_element_type=jnp.float32,
        )
        numerator = numerator + jnp.einsum(
            "shj,sjhd->shd",
            fresh_weights.astype(jnp.bfloat16),
            mixer_new_values,
            preferred_element_type=jnp.float32,
        )
        attended = numerator / weight_sum[:, :, None]
        mixed_heads = (
            (rms_scale(readout, gain_head[None]) + attended)
            .astype(jnp.bfloat16)
            .reshape(slot_count, local_width)
        )
        partial_out = jnp.dot(mixed_heads, w_out[0], preferred_element_type=jnp.float32)
        mixer_out = lax.psum(partial_out, "head")
        stream_out = (stream_in.astype(jnp.float32) + mixer_out).astype(jnp.bfloat16)
        mixer_history = jnp.concatenate([mixer_history[:, 1:], projected[:, None]], axis=1)
        stream_out, next_history, next_state, next_keys, next_values = (
            stream_out,
            mixer_history,
            mixer_delta_state,
            mixer_new_keys,
            mixer_new_values,
        )
        history = jnp.where(is_valid, next_history, history)
        delta_state = jnp.where(is_valid, next_state, delta_state)
        new_keys = jnp.where(is_valid, next_keys, new_keys)
        new_values = jnp.where(is_valid, next_values, new_values)
        stored = lax.dynamic_update_slice_in_dim(produced, stream_out[:, None], t_index, 1)
        produced = jnp.where(is_valid, stored, produced)
        if position < token_count:
            received = passed_along(stream_out, "section", 1)
    return (produced[None], delta_state[None])


def solution(mesh):
    return jax.shard_map(
        shards,
        mesh=mesh,
        in_specs=(
            P("req", None),
            P(),
            P(),
            P(("req", "head"), None),
            P("section", None, "req", None, "head"),
            P("section", None, "req", "head", None),
            P("section", "req", None, None, "head"),
            P("section", "req", None, None, "head"),
            P("section", None, None, "head"),
            P("section", "head", None),
            P("section", None, "head"),
            P("section", None, None, "head"),
            P("section", None),
            P("section", "head"),
            P("section", "head"),
        ),
        out_specs=(P("section", "req", None, None), P("section", "req", None, "head", None)),
        check_vma=False,
    )
```

profile of v0, /device:TPU:2, one launch (start us, length us, event | category | flops | bytes accessed | tf_op | source)
XLA Modules:
  0.0 1202.1 jit_solution(7097759639940147544)
XLA Ops:
  7.4 11.5 all-to-all-start
  18.9 66.6 %all-gather = s32[32,4,4]{2,1,0:T(4,128)S(1)} all-gather(s32[1,4,4]{2,1,0:T(4,128)S(1)} %bitcast.617), channel_id=1, replica_groups=mesh['section'=2,'req'=32,'head'=4] {'req'}, dimensions={0}, use_global_device_ids=true | all-gather | bytes 2112 | tf_op jit(solution)/shard_map/all_gather | solution.py:52
  85.6 4.1 fusion.75
  92.9 5.1 gather_fusion.2
  98.0 4.7 fusion
  103.7 8.2 all-to-all-start.1
  111.9 792.8 %all-reduce.1 = bf16[512,2048]{1,0:T(8,128)(2,1)} all-reduce(f32[512,2048]{1,0:T(8,128)} %fusion.75), channel_id=1, replica_groups=mesh['section'=2,'req'=32,'head'=4] {'req','head'}, use_global_device_ids=true, to_apply=%region_0.0 | all-reduce | flops 1048576 | bytes 6291456 | tf_op jit(solution)/shard_map/psum | solution.py:58
  905.6 8.8 copy.140
  915.4 4.5 convolution_convert_fusion.4
  934.9 4.2 copy.145
  941.5 4.2 copy.146
  948.7 20.5 %psum.43 = f32[4,2048]{1,0:T(4,128)S(1)} all-reduce(f32[4,2048]{1,0:T(4,128)S(1)} %fusion.9), channel_id=1, replica_groups=mesh['section'=2,'req'=32,'head'=4] {'head'}, use_global_device_ids=true, to_apply=%region_12.13 | all-reduce | flops 8192 | bytes 65536 | tf_op jit(solution)/shard_map/psum | solution.py:192
  978.5 4.5 convolution_convert_fusion.3
  1005.6 15.6 %psum.44 = f32[4,2048]{1,0:T(4,128)} all-reduce(f32[4,2048]{1,0:T(4,128)} %fusion.7), channel_id=1, replica_groups=mesh['section'=2,'req'=32,'head'=4] {'head'}, use_global_device_ids=true, to_apply=%region_24.25 | all-reduce | flops 8192 | bytes 65536 | tf_op jit(solution)/shard_map/psum | solution.py:192
  1033.1 4.5 convolution_convert_fusion.2
  1062.5 16.8 %psum.45 = f32[4,2048]{1,0:T(4,128)} all-reduce(f32[4,2048]{1,0:T(4,128)S(1)} %fusion.5), channel_id=1, replica_groups=mesh['section'=2,'req'=32,'head'=4] {'head'}, use_global_device_ids=true, to_apply=%region_36.37 | all-reduce | flops 8192 | bytes 65536 | tf_op jit(solution)/shard_map/psum | solution.py:192
  1092.9 4.5 convolution_convert_fusion.1
  1115.6 3.4 fusion.31
  1121.9 15.6 %psum.46 = f32[4,2048]{1,0:T(4,128)} all-reduce(f32[4,2048]{1,0:T(4,128)} %fusion.3), channel_id=1, replica_groups=mesh['section'=2,'req'=32,'head'=4] {'head'}, use_global_device_ids=true, to_apply=%region_48.49 | all-reduce | flops 8192 | bytes 65536 | tf_op jit(solution)/shard_map/psum | solution.py:192
  1146.6 4.5 convolution_convert_fusion
  1166.7 3.6 fusion.39
  1172.0 3.4 fusion.26
  1177.1 16.8 %psum.47 = f32[4,2048]{1,0:T(4,128)} all-reduce(f32[4,2048]{1,0:T(4,128)S(1)} %fusion.1), channel_id=1, replica_groups=mesh['section'=2,'req'=32,'head'=4] {'head'}, use_global_device_ids=true, to_apply=%region_60.61 | all-reduce | flops 8192 | bytes 65536 | tf_op jit(solution)/shard_map/psum | solution.py:192
  1196.8 5.1 add_select_fusion
  (515 shorter events, 166.1 us)
Async XLA Ops:
  0.6 947.7 %copy-start = (bf16[1,512,2048]{2,1,0:T(8,128)(2,1)S(1)}, bf16[1,512,2048]{2,1,0:T(8,128)(2,1)}, u32[]{:S(2)}) copy-start(bf16[1,512,2048]{2,1,0:T(8,128)(2,1)} %param.24) | copy-start | bytes 6291460
  6.1 12.8 %copy-start.117 = (s32[4,4]{1,0:T(4,128)S(1)}, s32[4,4]{1,0:T(4,128)}, u32[]{:S(2)}) copy-start(s32[4,4]{1,0:T(4,128)} %param.15) | copy-start | bytes 196
  7.4 95.3 %all-to-all-start = ((f32[1,128,4,4,128]{4,3,2,0,1:T(4,128)}), f32[1,128,4,4,128]{4,3,2,0,1:T(4,128)S(1)}, u32[]{:S(2)}, u32[]{:S(2)}) async-start(f32[1,128,4,4,128]{4,3,2,0,1:T(4,128)} %bitcast_select_fusion.1), calls=%async_computation | async-start | bytes 2097152 | tf_op jit(solution)/shard_map/all_to_all | solution.py:64
  103.7 826.0 %all-to-all-start.1 = ((bf16[1,128,16,2,512]{4,2,3,0,1:T(8,128)(2,1)}), bf16[1,128,16,2,512]{4,2,3,0,1:T(8,128)(2,1)}, u32[]{:S(2)}, u32[]{:S(2)}) async-start(bf16[1,128,16,2,512]{4,2,3,0,1:T(8,128)(2,1)} %fusion), calls=%async_computation.1 | async-start | bytes 8388608 | tf_op jit(solution)/shard_map/all_to_all | solution.py:68
  111.8 792.8 %copy-start.11 = (bf16[1,4,3,3,512]{4,1,3,2,0:T(4,128)(2,1)S(1)}, bf16[1,4,3,3,512]{4,1,3,2,0:T(4,128)(2,1)}, u32[]{:S(2)}) copy-start(bf16[1,4,3,3,512]{4,1,3,2,0:T(4,128)(2,1)} %param.21) | copy-start | bytes 110596
  111.8 792.8 %copy-start.80 = (f32[1,4,3,512]{3,1,2,0:T(4,128)S(1)}, f32[1,4,3,512]{3,1,2,0:T(4,128)}, u32[]{:S(2)}) copy-start(f32[1,4,3,512]{3,1,2,0:T(4,128)} %param.26) | copy-start | bytes 73732
  922.2 25.9 %copy-start.87 = (bf16[4,4,512]{2,1,0:T(4,128)(2,1)}, bf16[4,4,512]{2,1,0:T(4,128)(2,1)S(1)}, u32[]{:S(2)}) copy-start(bf16[4,4,512]{2,1,0:T(4,128)(2,1)S(1)} %get-tuple-element.16) | copy-start | bytes 49156
  925.9 57.2 %copy-start.8 = (bf16[4,3,3,512]{3,0,2,1:T(4,128)(2,1)}, bf16[4,3,3,512]{3,0,2,1:T(4,128)(2,1)S(1)}, u32[]{:S(2)}) copy-start(bf16[4,3,3,512]{3,0,2,1:T(4,128)(2,1)S(1)} %maximum_select_fusion) | copy-start | bytes 110596
  969.9 7.7 collective-permute-start
  984.3 16.2 %copy-start.30 = (f32[4,4,128]{2,1,0:T(4,128)S(1)}, f32[4,4,128]{2,1,0:T(4,128)}, u32[]{:S(2)}) copy-start(f32[4,4,128]{2,1,0:T(4,128)} %copy-done.29) | copy-start | bytes 24580
  984.3 16.2 %copy-start.35 = (f32[4,128,4]{1,2,0:T(4,128)S(1)}, f32[4,128,4]{1,2,0:T(4,128)}, u32[]{:S(2)}) copy-start(f32[4,128,4]{1,2,0:T(4,128)} %copy-done.34) | copy-start | bytes 24580
  985.1 17.6 %copy-start.64 = (f32[4,128,4]{1,2,0:T(4,128)}, f32[4,128,4]{1,2,0:T(4,128)S(1)}, u32[]{:S(2)}) copy-start(f32[4,128,4]{1,2,0:T(4,128)S(1)} %fusion.317) | copy-start | bytes 24580
  1002.9 18.3 %slice-start = ((bf16[4,3,3,512]{3,0,2,1:T(4,128)(2,1)}), bf16[4,2,3,512]{3,0,2,1:T(4,128)(2,1)S(1)}, s32[]{:S(2)}) async-start(bf16[4,3,3,512]{3,0,2,1:T(4,128)(2,1)} %copy-done.8), calls=%async_computation.2 | async-start | bytes 49152 | tf_op jit(solution)/shard_map/slice | solution.py:194
  1002.9 18.3 %copy-start.25 = (bf16[4,1536]{1,0:T(4,128)(2,1)S(1)}, bf16[4,1536]{1,0:T(4,128)(2,1)}, u32[]{:S(2)}) copy-start(bf16[4,1536]{1,0:T(4,128)(2,1)} %copy-done.24) | copy-start | bytes 36868
  1023.2 7.5 collective-permute-start.1
  1037.7 17.7 %copy-start.31 = (f32[4,4,128]{2,1,0:T(4,128)S(1)}, f32[4,4,128]{2,1,0:T(4,128)}, u32[]{:S(2)}) copy-start(f32[4,4,128]{2,1,0:T(4,128)} %copy-done.29) | copy-start | bytes 24580
  1080.1 17.3 %copy-start.9 = (bf16[4,3,3,512]{3,0,2,1:T(4,128)(2,1)}, bf16[4,3,3,512]{3,0,2,1:T(4,128)(2,1)S(1)}, u32[]{:S(2)}) copy-start(bf16[4,3,3,512]{3,0,2,1:T(4,128)(2,1)S(1)} %maximum_select_fusion.2) | copy-start | bytes 110596
  1081.5 8.9 collective-permute-start.2
  1119.2 18.3 %slice-start.1 = ((bf16[4,3,3,512]{3,0,2,1:T(4,128)(2,1)}), bf16[4,2,3,512]{3,0,2,1:T(4,128)(2,1)S(1)}, s32[]{:S(2)}) async-start(bf16[4,3,3,512]{3,0,2,1:T(4,128)(2,1)} %copy-done.9), calls=%async_computation.3 | async-start | bytes 49152 | tf_op jit(solution)/shard_map/slice | solution.py:194
  1119.2 18.3 %copy-start.27 = (bf16[4,1536]{1,0:T(4,128)(2,1)S(1)}, bf16[4,1536]{1,0:T(4,128)(2,1)}, u32[]{:S(2)}) copy-start(bf16[4,1536]{1,0:T(4,128)(2,1)} %copy-done.26) | copy-start | bytes 36868
  1139.0 6.7 collective-permute-start.3
  1175.7 21.1 %copy-start.5 = (f32[1,4,32,4,4,128]{5,4,3,2,1,0:T(4,128)S(1)}, f32[1,4,32,4,4,128]{5,4,3,2,1,0:T(4,128)}, u32[]{:S(2)}) copy-start(f32[1,4,32,4,4,128]{5,4,3,2,1,0:T(4,128)} %copy.150) | copy-start | bytes 3145732
  1176.4 20.4 %copy-start.59 = (f32[4,4,128]{2,1,0:T(4,128)S(1)}, f32[4,4,128]{2,1,0:T(4,128)}, u32[]{:S(2)}) copy-start(f32[4,4,128]{2,1,0:T(4,128)} %copy-done.56) | copy-start | bytes 24580
  1176.4 20.4 %copy-start.62 = (f32[4,4,128]{2,1,0:T(4,128)S(1)}, f32[4,4,128]{2,1,0:T(4,128)}, u32[]{:S(2)}) copy-start(f32[4,4,128]{2,1,0:T(4,128)} %copy-done.60) | copy-start | bytes 24580
  (105 other events, 385.1 us)
where the time goes:
time: 1210 us; the launch traced here: 1200 us
  blocking collectives  945 us (78%)
  matrix products  81.3 us (7%)
  local copies, waits for them, and re-layouts  76.8 us (6%)
  other arithmetic  69.3 us (6%)
  starting transfers between devices  27.5 us (2%)
    psum x1, blocking collectives, shards(): summed = lax.psum(looked_up, ('req', 'head'))  793 us
    psum x5, blocking collectives, shards(): mixer_out = lax.psum(partial_out, 'head')  85.3 us
    all_gather x1, blocking collectives, shards(): all_ids = lax.all_gather(token_ids, 'req', axis=0, tiled=True)  66.6 us
  transfers between devices with their start and end apart: 6, of which 0 were waited for; matrix products, arithmetic and copies ran while one was open for 5% of the time, Pallas kernels for 0%

commit v1 on v0

--- a/solution.py
+++ b/solution.py
@@ -55,7 +55,8 @@
         all_ids.reshape(-1)[:, None] == first_row + jnp.arange(vocab_dev, dtype=jnp.int32)[None, :]
     ).astype(jnp.bfloat16)
     looked_up = jnp.dot(onehot, embed_table, preferred_element_type=jnp.float32)
-    summed = lax.psum(looked_up, ("req", "head"))
+    inner = lax.psum(looked_up, "req")
+    summed = lax.psum(inner, "head")
     own_rows = lax.dynamic_slice_in_dim(
         summed, group_index * slot_count * token_count, slot_count * token_count, 0
     )

time: 1210 us -> 641 us (0.53)
  blocking collectives: 945 us -> 206 us
  waiting for transfers between devices: 0.02 us -> 156 us
  between operations: 2.47 us -> 15.9 us
    psum x1, blocking collectives: 793 us -> 74.2 us  [shards(): summed = lax.psum(inner, 'head')]
    psum x0 -> x1, waiting for transfers between devices: none -> 154 us  [shards(): inner = lax.psum(looked_up, 'req')]
    all_gather x1, blocking collectives: 66.6 us -> 52.3 us  [shards(): all_ids = lax.all_gather(token_ids, 'req', axis=0, tiled=True)]
    unnamed x252 -> x248, local copies, waits for them, and re-layouts: 23.8 us -> 26.5 us
  transfers between devices with their start and end apart: 6 -> 7, of which waited for: 0 -> 2; matrix products, arithmetic and copies ran while one was open for 5% -> 11% of each run, Pallas kernels for 0% -> 0%
where the time goes in v1:
time: 641 us; the launch traced here: 629 us
  blocking collectives  206 us (32%)
  waiting for transfers between devices  156 us (24%)
  matrix products  82 us (13%)
  local copies, waits for them, and re-layouts  79.1 us (12%)
  other arithmetic  68.3 us (11%)
  starting transfers between devices  22.4 us (3%)
  between operations  15.9 us (2%)
    psum x1, waiting for transfers between devices, shards(): inner = lax.psum(looked_up, 'req')  154 us
    psum x5, blocking collectives, shards(): mixer_out = lax.psum(partial_out, 'head')  79.2 us
    psum x1, blocking collectives, shards(): summed = lax.psum(inner, 'head')  74.2 us
    all_gather x1, blocking collectives, shards(): all_ids = lax.all_gather(token_ids, 'req', axis=0, tiled=True)  52.3 us
    unnamed x248, local copies, waits for them, and re-layouts  26.5 us
    dot_general x5, matrix products, shards(): jnp.dot(normed, qkv_matrix, preferred_element_type=jnp.float32)  22.5 us
    dot_general x5, matrix products, shards(): jnp.einsum('skhv,shk->shv', mixer_delta_state, query_vec, precision=lax.P...  12.9 us
  transfers between devices with their start and end apart: 7, of which 2 were waited for; matrix products, arithmetic and copies ran while one was open for 11% of the time, Pallas kernels for 0%

profile of v1, /device:TPU:2, one launch (start us, length us, event | category | flops | bytes accessed | tf_op | source)
XLA Modules:
  0.0 629.0 jit_solution(11567480472478218798)
XLA Ops:
  7.2 52.3 %all-gather = s32[32,4,4]{2,1,0:T(4,128)S(1)} all-gather(s32[1,4,4]{2,1,0:T(4,128)} %bitcast.617), channel_id=1, replica_groups=mesh['section'=2,'req'=32,'head'=4] {'req'}, dimensions={0}, use_global_device_ids=true | all-gather | bytes 2112 | tf_op jit(solution)/shard_map/all_gather | solution.py:52
  59.6 4.1 fusion.75
  69.3 6.1 all-to-all-start
  75.6 5.3 copy.413
  80.8 5.1 gather_fusion.2
  85.9 8.8 %copy.140 = bf16[1,2048,3,512]{1,3,2,0:T(8,128)(2,1)} copy(bf16[1,2048,3,512]{3,1,2,0:T(8,128)(2,1)} %param.23) | data formatting | bytes 12582912 | tf_op args[8]
  99.1 4.7 fusion
  106.3 8.4 %all-to-all-start.1 = ((bf16[1,128,16,2,512]{4,2,3,0,1:T(8,128)(2,1)}), bf16[1,128,16,2,512]{4,2,3,0,1:T(8,128)(2,1)}, u32[]{:S(2)}, u32[]{:S(2)}) async-start(bf16[1,128,16,2,512]{4,2,3,0,1:T(8,128)(2,1)} %fusion), calls=%async_computation.1 | async-start | bytes 8388608 | tf_op jit(solution)/shard_map/all_to_all | solution.py:69
  117.9 154.1 %all-reduce.3.cloned.1.call-done = f32[512,2048]{1,0:T(8,128)} async-done(((f32[512,2048]{1,0:T(8,128)}), f32[512,2048]{1,0:T(8,128)}) %all-reduce.3.cloned.1.call-update) | async-done | bytes 4194320 | tf_op jit(solution)/shard_map/psum | solution.py:58
  272.0 74.2 %all-reduce.4 = bf16[512,2048]{1,0:T(8,128)(2,1)} all-reduce(f32[512,2048]{1,0:T(8,128)} %all-reduce.3.cloned.1.call-done), channel_id=1, replica_groups=mesh['section'=2,'req'=32,'head'=4] {'head'}, use_global_device_ids=true, to_apply=%region_1.0 | all-reduce | flops 1048576 | bytes 6291456 | tf_op jit(solution)/shard_map/psum | solution.py:59
  347.9 4.5 convolution_convert_fusion.4
  361.4 4.2 copy.145
  368.0 4.2 copy.146
  375.2 14.0 %psum.51 = f32[4,2048]{1,0:T(4,128)S(1)} all-reduce(f32[4,2048]{1,0:T(4,128)S(1)} %fusion.9), channel_id=1, replica_groups=mesh['section'=2,'req'=32,'head'=4] {'head'}, use_global_device_ids=true, to_apply=%region_13.14 | all-reduce | flops 8192 | bytes 65536 | tf_op jit(solution)/shard_map/psum | solution.py:193
  398.4 4.5 convolution_convert_fusion.3
  425.3 17.8 %psum.52 = f32[4,2048]{1,0:T(4,128)} all-reduce(f32[4,2048]{1,0:T(4,128)} %fusion.7), channel_id=1, replica_groups=mesh['section'=2,'req'=32,'head'=4] {'head'}, use_global_device_ids=true, to_apply=%region_25.26 | all-reduce | flops 8192 | bytes 65536 | tf_op jit(solution)/shard_map/psum | solution.py:193
  455.0 4.5 convolution_convert_fusion.2
  484.3 14.9 %psum.53 = f32[4,2048]{1,0:T(4,128)} all-reduce(f32[4,2048]{1,0:T(4,128)S(1)} %fusion.5), channel_id=1, replica_groups=mesh['section'=2,'req'=32,'head'=4] {'head'}, use_global_device_ids=true, to_apply=%region_37.38 | all-reduce | flops 8192 | bytes 65536 | tf_op jit(solution)/shard_map/psum | solution.py:193
  512.8 4.5 convolution_convert_fusion.1
  541.9 17.5 %psum.54 = f32[4,2048]{1,0:T(4,128)} all-reduce(f32[4,2048]{1,0:T(4,128)} %fusion.3), channel_id=1, replica_groups=mesh['section'=2,'req'=32,'head'=4] {'head'}, use_global_device_ids=true, to_apply=%region_49.50 | all-reduce | flops 8192 | bytes 65536 | tf_op jit(solution)/shard_map/psum | solution.py:193
  568.5 4.5 convolution_convert_fusion
  588.6 3.6 fusion.39
  599.0 14.9 %psum.55 = f32[4,2048]{1,0:T(4,128)} all-reduce(f32[4,2048]{1,0:T(4,128)S(1)} %fusion.1), channel_id=1, replica_groups=mesh['section'=2,'req'=32,'head'=4] {'head'}, use_global_device_ids=true, to_apply=%region_61.62 | all-reduce | flops 8192 | bytes 65536 | tf_op jit(solution)/shard_map/psum | solution.py:193
  616.8 5.1 add_select_fusion
  (514 shorter events, 171.4 us)
Async XLA Ops:
  7.2 367.7 %copy-start = (bf16[1,512,2048]{2,1,0:T(8,128)(2,1)S(1)}, bf16[1,512,2048]{2,1,0:T(8,128)(2,1)}, u32[]{:S(2)}) copy-start(bf16[1,512,2048]{2,1,0:T(8,128)(2,1)} %param.24) | copy-start | bytes 6291460
  7.2 264.8 %all-reduce.3.cloned.1.call-start = ((), (), s32[]{:S(2)}) async-start(), calls=%async_computation.2 | async-start | bytes 8388608 | tf_op jit(solution)/shard_map/psum | solution.py:58
  69.3 36.0 %all-to-all-start = ((f32[1,128,4,4,128]{4,3,2,0,1:T(4,128)}), f32[1,128,4,4,128]{4,3,2,0,1:T(4,128)S(1)}, u32[]{:S(2)}, u32[]{:S(2)}) async-start(f32[1,128,4,4,128]{4,3,2,0,1:T(4,128)} %bitcast_select_fusion.1), calls=%async_computation | async-start | bytes 2097152 | tf_op jit(solution)/shard_map/all_to_all | solution.py:65
  97.1 258.6 %copy-start.91 = (bf16[4,4,512]{2,1,0:T(4,128)(2,1)}, bf16[4,4,512]{2,1,0:T(4,128)(2,1)S(1)}, u32[]{:S(2)}) copy-start(bf16[4,4,512]{2,1,0:T(4,128)(2,1)S(1)} %get-tuple-element.17) | copy-start | bytes 49156
  97.1 277.5 %copy-start.86 = (bf16[4,4,512]{2,1,0:T(4,128)(2,1)}, bf16[4,4,512]{2,1,0:T(4,128)(2,1)S(1)}, u32[]{:S(2)}) copy-start(bf16[4,4,512]{2,1,0:T(4,128)(2,1)S(1)} %get-tuple-element.16) | copy-start | bytes 49156
  106.3 249.9 %all-to-all-start.1 = ((bf16[1,128,16,2,512]{4,2,3,0,1:T(8,128)(2,1)}), bf16[1,128,16,2,512]{4,2,3,0,1:T(8,128)(2,1)}, u32[]{:S(2)}, u32[]{:S(2)}) async-start(bf16[1,128,16,2,512]{4,2,3,0,1:T(8,128)(2,1)} %fusion), calls=%async_computation.1 | async-start | bytes 8388608 | tf_op jit(solution)/shard_map/all_to_all | solution.py:69
  117.9 230.0 %copy-start.12 = (f32[1,2048]{1,0:T(1,128)S(1)}, f32[1,2048]{1,0:T(1,128)}, u32[]{:S(2)}) copy-start(f32[1,2048]{1,0:T(1,128)} %param.27) | copy-start | bytes 24580
  356.2 46.8 %copy-start.8 = (bf16[4,3,3,512]{3,0,2,1:T(4,128)(2,1)}, bf16[4,3,3,512]{3,0,2,1:T(4,128)(2,1)S(1)}, u32[]{:S(2)}) copy-start(bf16[4,3,3,512]{3,0,2,1:T(4,128)(2,1)S(1)} %maximum_select_fusion) | copy-start | bytes 110596
  389.9 6.2 collective-permute-start
  404.2 16.0 %copy-start.29 = (f32[4,4,128]{2,1,0:T(4,128)S(1)}, f32[4,4,128]{2,1,0:T(4,128)}, u32[]{:S(2)}) copy-start(f32[4,4,128]{2,1,0:T(4,128)} %copy-done.28) | copy-start | bytes 24580
  404.2 16.0 %copy-start.34 = (f32[4,128,4]{1,2,0:T(4,128)S(1)}, f32[4,128,4]{1,2,0:T(4,128)}, u32[]{:S(2)}) copy-start(f32[4,128,4]{1,2,0:T(4,128)} %copy-done.33) | copy-start | bytes 24580
  405.0 17.5 %copy-start.63 = (f32[4,128,4]{1,2,0:T(4,128)}, f32[4,128,4]{1,2,0:T(4,128)S(1)}, u32[]{:S(2)}) copy-start(f32[4,128,4]{1,2,0:T(4,128)S(1)} %fusion.317) | copy-start | bytes 24580
  422.6 20.5 %slice-start = ((bf16[4,3,3,512]{3,0,2,1:T(4,128)(2,1)}), bf16[4,2,3,512]{3,0,2,1:T(4,128)(2,1)S(1)}, s32[]{:S(2)}) async-start(bf16[4,3,3,512]{3,0,2,1:T(4,128)(2,1)} %copy-done.8), calls=%async_computation.3 | async-start | bytes 49152 | tf_op jit(solution)/shard_map/slice | solution.py:195
  422.6 20.5 %copy-start.24 = (bf16[4,1536]{1,0:T(4,128)(2,1)S(1)}, bf16[4,1536]{1,0:T(4,128)(2,1)}, u32[]{:S(2)}) copy-start(bf16[4,1536]{1,0:T(4,128)(2,1)} %copy-done.23) | copy-start | bytes 36868
  445.1 7.5 %collective-permute-start.1 = (bf16[4,2048]{1,0:T(4,128)(2,1)}, bf16[4,2048]{1,0:T(4,128)(2,1)}, u32[]{:S(2)}, u32[]{:S(2)}) collective-permute-start(bf16[4,2048]{1,0:T(4,128)(2,1)} %get-tuple-element.57), channel_id=1, source_target_pairs={{0,128},{1,129},{2,130},{3,131},{4,132},{5,133},{6,134},{7,135},{8... | collective-permute-start | bytes 49160 | tf_op jit(solution)/shard_map/ppermute | solution.py:14
  459.6 17.5 %copy-start.30 = (f32[4,4,128]{2,1,0:T(4,128)S(1)}, f32[4,4,128]{2,1,0:T(4,128)}, u32[]{:S(2)}) copy-start(f32[4,4,128]{2,1,0:T(4,128)} %copy-done.28) | copy-start | bytes 24580
  500.0 17.3 %copy-start.9 = (bf16[4,3,3,512]{3,0,2,1:T(4,128)(2,1)}, bf16[4,3,3,512]{3,0,2,1:T(4,128)(2,1)S(1)}, u32[]{:S(2)}) copy-start(bf16[4,3,3,512]{3,0,2,1:T(4,128)(2,1)S(1)} %maximum_select_fusion.2) | copy-start | bytes 110596
  501.4 8.9 %collective-permute-start.2 = (bf16[4,2048]{1,0:T(4,128)(2,1)}, bf16[4,2048]{1,0:T(4,128)(2,1)}, u32[]{:S(2)}, u32[]{:S(2)}) collective-permute-start(bf16[4,2048]{1,0:T(4,128)(2,1)} %get-tuple-element.51), channel_id=1, source_target_pairs={{0,128},{1,129},{2,130},{3,131},{4,132},{5,133},{6,134},{7,135},{8... | collective-permute-start | bytes 49160 | tf_op jit(solution)/shard_map/ppermute | solution.py:14
  539.2 20.2 %slice-start.1 = ((bf16[4,3,3,512]{3,0,2,1:T(4,128)(2,1)}), bf16[4,2,3,512]{3,0,2,1:T(4,128)(2,1)S(1)}, s32[]{:S(2)}) async-start(bf16[4,3,3,512]{3,0,2,1:T(4,128)(2,1)} %copy-done.9), calls=%async_computation.4 | async-start | bytes 49152 | tf_op jit(solution)/shard_map/slice | solution.py:195
  539.2 20.2 %copy-start.26 = (bf16[4,1536]{1,0:T(4,128)(2,1)S(1)}, bf16[4,1536]{1,0:T(4,128)(2,1)}, u32[]{:S(2)}) copy-start(bf16[4,1536]{1,0:T(4,128)(2,1)} %copy-done.25) | copy-start | bytes 36868
  560.8 6.7 %collective-permute-start.3 = (bf16[4,2048]{1,0:T(4,128)(2,1)S(1)}, bf16[4,2048]{1,0:T(4,128)(2,1)}, u32[]{:S(2)}, u32[]{:S(2)}) collective-permute-start(bf16[4,2048]{1,0:T(4,128)(2,1)S(1)} %get-tuple-element.45), channel_id=1, source_target_pairs={{0,128},{1,129},{2,130},{3,131},{4,132},{5,133},{6,134},{7,135},{8... | collective-permute-start | bytes 49160 | tf_op jit(solution)/shard_map/ppermute | solution.py:14
  597.6 19.2 %copy-start.6 = (f32[1,4,32,4,4,128]{5,4,3,2,1,0:T(4,128)S(1)}, f32[1,4,32,4,4,128]{5,4,3,2,1,0:T(4,128)}, u32[]{:S(2)}) copy-start(f32[1,4,32,4,4,128]{5,4,3,2,1,0:T(4,128)} %copy.150) | copy-start | bytes 3145732
  598.3 18.5 %copy-start.58 = (f32[4,4,128]{2,1,0:T(4,128)S(1)}, f32[4,4,128]{2,1,0:T(4,128)}, u32[]{:S(2)}) copy-start(f32[4,4,128]{2,1,0:T(4,128)} %copy-done.55) | copy-start | bytes 24580
  598.3 18.5 %copy-start.61 = (f32[4,4,128]{2,1,0:T(4,128)S(1)}, f32[4,4,128]{2,1,0:T(4,128)}, u32[]{:S(2)}) copy-start(f32[4,4,128]{2,1,0:T(4,128)} %copy-done.59) | copy-start | bytes 24580
  (104 other events, 372.2 us)
Sparse Core Ops, SparseCore 0:
  63.8 208.0 all-reduce.2
